TPU v7x, 512 devices: a whole 4x8x8 slice. The times are simulated.
512 devices in a mesh: dp: 32 (over z, y_lo, core), feat: 16 (over y_hi, x).
Axes of the slice: x: 4, y: 8 (y_hi: 4, y_lo: 2; y = y_hi * 2 + y_lo), z: 8, core: 2. Of those that a mesh axis runs over, the one named last changes fastest.
Arguments:
- tokens: bfloat16 [8192, 8192], P('dp', 'feat'), may hold values from -6 to 6
- up_left: bfloat16 [16, 512, 2048], P('feat', 'dp'), may hold values from -0.25 to 0.25
- up_right: bfloat16 [2048, 16, 16], P('feat'), may hold values from -1.5 to 1.5
- down_left: bfloat16 [16, 2048, 512], P('feat', 'dp'), may hold values from -0.125 to 0.125
- down_right: bfloat16 [512, 16, 16], P('feat'), may hold values from -1.5 to 1.5
- layer_grad: bfloat16 [8192, 8192], P('dp', 'feat'), may hold values from -6 to 6
Outputs:
- layer_out: bfloat16 [8192, 8192], P('dp', 'feat')
- grad_tokens: bfloat16 [8192, 8192], P('dp', 'feat')
- grad_up_left: float32 [16, 512, 2048], P('feat', 'dp')
- grad_up_right: float32 [2048, 16, 16], P('feat')
- grad_down_left: float32 [16, 2048, 512], P('feat', 'dp')
- grad_down_right: float32 [512, 16, 16], P('feat')
All inputs are finite; a program needn't handle non-finite values.
Results may differ from a plain program's by a relative error of at most 0.0067.
Values may be sent and summed in bfloat16 or wider, within the bound.
No kernel may reach another device: no remote copies, remote signals or barrier semaphores. Data moves between devices by JAX's collectives and lax.ppermute only.
A program may use at most 128 MiB of HBM per device.

v0:
```python
import jax
import jax.numpy as jnp
import numpy as np
from jax import lax
from jax.sharding import Mesh
from jax.sharding import PartitionSpec as P

TILE_UP = 128
TILE_DOWN = 32
DP_AXES = ("z", "ylo", "core")
FEAT_AXES = ("yhi", "x")


def split_mesh(mesh):
    n_dp = mesh.shape["dp"]
    n_feat = mesh.shape["feat"]
    sizes = (n_dp // 4, 2, 2, n_feat // 4, 4)
    devices = np.asarray(mesh.devices).reshape(sizes)
    return Mesh(devices, DP_AXES + FEAT_AXES)


def exchange(wired):
    rows, feat_count, piece = wired.shape
    n_x = lax.axis_size("x")
    n_y = feat_count // n_x
    shaped = wired.reshape(rows, n_y, n_x, piece)
    shaped = lax.all_to_all(shaped, "x", 2, 2, tiled=True)
    shaped = lax.all_to_all(shaped, "yhi", 1, 1, tiled=True)
    return shaped.reshape(rows, feat_count, piece)


def dp_reduce_scatter(part, row_axis):
    shape = part.shape
    rows = shape[row_axis]
    n_z = lax.axis_size("z")
    split = shape[:row_axis] + (n_z, 2, 2, rows // (4 * n_z)) + shape[row_axis + 1 :]
    x = part.reshape(split)
    x = lax.psum_scatter(x, "core", scatter_dimension=row_axis + 2, tiled=True)
    x = lax.psum_scatter(x, "z", scatter_dimension=row_axis, tiled=True)
    x = lax.psum_scatter(x, "ylo", scatter_dimension=row_axis + 1, tiled=True)
    return x.reshape(shape[:row_axis] + (rows // (4 * n_z),) + shape[row_axis + 1 :])


def dp_all_gather(local, row_axis):
    shape = local.shape
    rows = shape[row_axis]
    x = local.reshape(shape[:row_axis] + (1, 1, 1, rows) + shape[row_axis + 1 :])
    x = lax.all_gather(x, "ylo", axis=row_axis + 1, tiled=True)
    x = lax.all_gather(x, "z", axis=row_axis, tiled=True)
    x = lax.all_gather(x, "core", axis=row_axis + 2, tiled=True)
    total = x.shape[row_axis] * x.shape[row_axis + 1] * x.shape[row_axis + 2] * rows
    return x.reshape(shape[:row_axis] + (total,) + shape[row_axis + 1 :])


def to_wire(blocks, feat_count):
    tok_rows, local_blocks, full_width = blocks.shape
    piece = full_width // feat_count
    shaped = blocks.reshape(tok_rows, local_blocks, feat_count, piece).transpose(0, 2, 1, 3)
    return shaped.reshape(tok_rows, feat_count, local_blocks * piece)


def from_wire(wired, local_blocks):
    tok_rows, feat_count, line_len = wired.shape
    piece = line_len // local_blocks
    shaped = wired.reshape(tok_rows, feat_count, local_blocks, piece).transpose(0, 2, 1, 3)
    return shaped.reshape(tok_rows, local_blocks, feat_count * piece)


def on_device(tokens, up_left, up_right, down_left, down_right, layer_grad):
    tok_rows = tokens.shape[0]
    local_blocks = up_left.shape[0]
    hidden_width = up_left.shape[2]
    block_width = down_left.shape[2]
    blocks_all = up_right.shape[1]
    group_up = up_right.shape[0]
    group_down = down_right.shape[0]
    feat_count = lax.axis_size("yhi") * lax.axis_size("x")
    n_dp = lax.axis_size("z") * lax.axis_size("ylo") * lax.axis_size("core")
    grad_scale = float(tok_rows * n_dp) ** (-0.5)
    tiles_up = group_up // TILE_UP
    tiles_down = group_down // TILE_DOWN
    up_full = dp_all_gather(up_left, 1)
    token_blocks = tokens.reshape(tok_rows, local_blocks, block_width)
    up_inner = jnp.einsum(
        "tbi,big->tbg", token_blocks, up_full, preferred_element_type=jnp.float32
    ).astype(jnp.bfloat16)
    up_mixed = exchange(to_wire(up_inner, feat_count))
    preact = jnp.einsum("tjg,gjk->tkg", up_mixed, up_right, preferred_element_type=jnp.float32)
    sigmoid_val = jax.nn.sigmoid(preact)
    activated = (
        (preact * sigmoid_val)
        .reshape(tok_rows, blocks_all, tiles_up, TILE_UP)
        .transpose(0, 2, 1, 3)
    )
    hidden = activated.reshape(tok_rows, local_blocks, hidden_width).astype(jnp.bfloat16)
    down_full = dp_all_gather(down_left, 1)
    down_inner = jnp.einsum(
        "tbh,bhc->tbc", hidden, down_full, preferred_element_type=jnp.float32
    ).astype(jnp.bfloat16)
    down_mixed = exchange(to_wire(down_inner, feat_count)).reshape(
        tok_rows, blocks_all * group_down
    )
    identity = jnp.eye(group_down, dtype=jnp.bfloat16).reshape(group_down, tiles_down, TILE_DOWN)
    mix_matrix = jnp.einsum(
        "cjk,cal->jcakl", down_right, identity, preferred_element_type=jnp.float32
    )
    mix_matrix = mix_matrix.astype(jnp.bfloat16).reshape(
        blocks_all * group_down, blocks_all * group_down
    )
    layer_out = jnp.dot(down_mixed, mix_matrix, preferred_element_type=jnp.float32).astype(
        jnp.bfloat16
    )
    grad_down_mixed = lax.dot_general(
        layer_grad, mix_matrix, (((1,), (1,)), ((), ())), preferred_element_type=jnp.float32
    ).astype(jnp.bfloat16)
    grad_by_group = layer_grad.reshape(tok_rows, tiles_down, blocks_all, TILE_DOWN).transpose(
        0, 2, 1, 3
    )
    grad_by_group = grad_by_group.reshape(tok_rows, blocks_all, group_down)
    right_down_term = (
        jnp.einsum(
            "tjc,tkc->cjk",
            down_mixed.reshape(tok_rows, blocks_all, group_down),
            grad_by_group,
            preferred_element_type=jnp.float32,
        )
        * grad_scale
    )
    grad_down_inner = from_wire(
        exchange(grad_down_mixed.reshape(tok_rows, feat_count, local_blocks * group_down)),
        local_blocks,
    )
    grad_down_left = dp_reduce_scatter(
        jnp.einsum("tbh,tbc->hbc", hidden, grad_down_inner, preferred_element_type=jnp.float32)
        * grad_scale,
        0,
    ).transpose(1, 0, 2)
    grad_hidden = jnp.einsum(
        "tbc,bhc->tbh", grad_down_inner, down_full, preferred_element_type=jnp.float32
    )
    grad_hidden = grad_hidden.reshape(tok_rows, tiles_up, blocks_all, TILE_UP).transpose(0, 2, 1, 3)
    grad_hidden = grad_hidden.reshape(tok_rows, blocks_all, group_up)
    grad_preact = (grad_hidden * sigmoid_val * (1.0 + preact * (1.0 - sigmoid_val))).astype(
        jnp.bfloat16
    )
    grad_up_mixed = jnp.einsum(
        "tkg,gjk->tjg", grad_preact, up_right, preferred_element_type=jnp.float32
    ).astype(jnp.bfloat16)
    right_up_term = (
        jnp.einsum("tjg,tkg->gjk", up_mixed, grad_preact, preferred_element_type=jnp.float32)
        * grad_scale
    )
    grad_up_inner = from_wire(exchange(grad_up_mixed), local_blocks)
    grad_tokens = jnp.einsum(
        "tbg,big->tbi", grad_up_inner, up_full, preferred_element_type=jnp.float32
    ).astype(jnp.bfloat16)
    grad_tokens = grad_tokens.reshape(tok_rows, local_blocks * block_width)
    grad_up_left = dp_reduce_scatter(
        jnp.einsum("tbi,tbg->ibg", token_blocks, grad_up_inner, preferred_element_type=jnp.float32)
        * grad_scale,
        0,
    ).transpose(1, 0, 2)
    rights = jnp.concatenate([right_up_term, right_down_term], axis=0)
    rights = lax.psum(rights, DP_AXES)
    grad_up_right = rights[:group_up]
    grad_down_right = rights[group_up:]
    return (layer_out, grad_tokens, grad_up_left, grad_up_right, grad_down_left, grad_down_right)


def solution(mesh):
    fine = split_mesh(mesh)
    row = P(DP_AXES, FEAT_AXES)
    weight = P(FEAT_AXES, DP_AXES, None)
    mixer = P(FEAT_AXES, None, None)
    return jax.shard_map(
        on_device,
        mesh=fine,
        in_specs=(row, weight, mixer, weight, mixer, row),
        out_specs=(row, row, weight, mixer, weight, mixer),
        check_vma=False,
    )
```

profile of v0, /device:TPU:1, one launch (start us, length us, event | category | flops | bytes accessed | tf_op | source)
XLA Modules:
  0.0 650.3 jit_solution(2913419054008153790)
XLA Ops:
  7.2 6.3 all-gather
  13.6 42.4 %all-gather.13.cloned.1.call-done = bf16[16,16,2048]{2,1,0:T(8,128)(2,1)} async-done(((bf16[2,16,2048]{2,1,0:T(8,128)(2,1)}), bf16[16,16,2048]{2,1,0:T(8,128)(2,1)}) %all-gather.13.cloned.1.call-update) | async-done | bytes 1048592 | tf_op jit(solution)/shard_map/all_gather | solution.py:49
  56.1 5.3 all-gather.2
  70.8 10.1 %all-gather.9.cloned.1.call-done = bf16[1,8,2,2,16,2048]{5,4,3,2,1,0:T(8,128)(2,1)} async-done(((bf16[1,8,2,1,16,2048]{5,4,3,2,1,0:T(8,128)(2,1)}), bf16[1,8,2,2,16,2048]{5,4,3,2,1,0:T(8,128)(2,1)}) %all-gather.9.cloned.1.call-update) | async-done | bytes 2097168 | tf_op jit(solution)/shard_map/all_gather | solution.py:50
  87.9 32.6 %all-gather.15.cloned.1.call-done = bf16[16,64,512]{2,1,0:T(8,128)(2,1)} async-done(((bf16[2,64,512]{2,1,0:T(8,128)(2,1)}), bf16[16,64,512]{2,1,0:T(8,128)(2,1)}) %all-gather.15.cloned.1.call-update) | async-done | bytes 1048592 | tf_op jit(solution)/shard_map/all_gather | solution.py:49
  121.3 6.5 all-to-all-start.5
  128.8 6.9 %all-to-all-done.5 = bf16[256,4,4,32]{0,3,2,1:T(8,128)(2,1)S(1)} async-done(((bf16[256,4,4,32]{0,3,2,1:T(8,128)(2,1)}), bf16[256,4,4,32]{0,3,2,1:T(8,128)(2,1)S(1)}, u32[]{:S(2)}, u32[]{:S(2)}) %all-to-all-start.5) | async-done | bytes 262176 | tf_op jit(solution)/shard_map/all_to_all | solution.py:28
  135.7 4.3 all-to-all-start.1
  141.2 4.1 all-gather.11.cloned.1.call-done
  147.6 18.1 %all-to-all-done.1 = bf16[256,4,4,128]{0,3,2,1:T(8,128)(2,1)} async-done(((bf16[256,4,4,128]{0,3,2,1:T(8,128)(2,1)}), bf16[256,4,4,128]{0,3,2,1:T(8,128)(2,1)}, u32[]{:S(2)}, u32[]{:S(2)}) %all-to-all-start.1) | async-done | bytes 1048608 | tf_op jit(solution)/shard_map/all_to_all | solution.py:28
  165.8 4.5 fusion.7
  172.3 15.0 %all_to_all.40 = bf16[256,4,4,128]{0,3,1,2:T(8,128)(2,1)S(1)} all-to-all(bf16[256,4,4,128]{0,3,1,2:T(8,128)(2,1)S(1)} %copy.95), channel_id=1, replica_groups=mesh['z'=8,'ylo'=2,'core'=2,'yhi'=4,'x'=4] {'x'}, dimensions={2} | all-to-all | bytes 2097152 | tf_op jit(solution)/shard_map/all_to_all | solution.py:27
  188.4 6.5 %all-to-all-start.7 = ((bf16[256,4,4,128]{0,3,2,1:T(8,128)(2,1)}), bf16[256,4,4,128]{0,3,2,1:T(8,128)(2,1)S(1)}, u32[]{:S(2)}, u32[]{:S(2)}) async-start(bf16[256,4,4,128]{0,3,2,1:T(8,128)(2,1)} %copy.96), calls=%async_computation.7 | async-start | bytes 2097152 | tf_op jit(solution)/shard_map/all_to_all | solution.py:28
  199.0 5.4 copy.103
  204.5 10.2 %all-to-all-done.7 = bf16[256,4,4,128]{0,3,2,1:T(8,128)(2,1)S(1)} async-done(((bf16[256,4,4,128]{0,3,2,1:T(8,128)(2,1)}), bf16[256,4,4,128]{0,3,2,1:T(8,128)(2,1)S(1)}, u32[]{:S(2)}, u32[]{:S(2)}) %all-to-all-start.7) | async-done | bytes 1048608 | tf_op jit(solution)/shard_map/all_to_all | solution.py:28
  218.7 53.0 %all-reduce.8.cloned.1.call-done = (f32[8,2,2,16,1,2048]{5,3,4,2,1,0:T(8,128)}, f32[8,2,2,64,1,512]{5,3,2,1,0,4:T(8,128)}) async-done(((f32[8,2,2,16,1,2048]{5,3,4,2,1,0:T(8,128)}, f32[8,2,2,64,1,512]{5,3,2,1,0,4:T(8,128)}), (f32[8,2,2,16,1,2048]{5,3,4,2,1,0:T(8,128)}, f32[8,2,2,64,1,512]{5,3,2,1,0,4:T(8,128)})) %all-reduce.8.cloned.1.call-update) | async-done | bytes 8388624
  283.2 9.2 %all_to_all.41 = bf16[256,4,4,32]{0,3,1,2:T(8,128)(2,1)S(1)} all-to-all(bf16[256,4,4,32]{0,3,1,2:T(8,128)(2,1)S(1)} %copy.87), channel_id=1, replica_groups=mesh['z'=8,'ylo'=2,'core'=2,'yhi'=4,'x'=4] {'x'}, dimensions={2} | all-to-all | bytes 524288 | tf_op jit(solution)/shard_map/all_to_all | solution.py:27
  293.1 6.5 all-to-all-start.3
  302.9 5.1 all-to-all-done.3
  309.3 7.6 %reduce-scatter.13.cloned.1.call-done = f32[1,2,1,64,1,512]{5,3,2,1,0,4:T(8,128)} async-done(((f32[8,2,1,64,1,512]{5,3,2,1,0,4:T(8,128)}), f32[1,2,1,64,1,512]{5,3,2,1,0,4:T(8,128)}) %reduce-scatter.13.cloned.1.call-update) | async-done | bytes 262160 | tf_op jit(solution)/shard_map/reduce_scatter | solution.py:39
  317.0 46.2 %reduce-scatter.9.cloned.1.call-done = f32[1,2,1,16,1,2048]{5,3,4,2,1,0:T(8,128)} async-done(((f32[8,2,1,16,1,2048]{5,3,4,2,1,0:T(8,128)}), f32[1,2,1,16,1,2048]{5,3,4,2,1,0:T(8,128)}) %reduce-scatter.9.cloned.1.call-update) | async-done | bytes 262160 | tf_op jit(solution)/shard_map/reduce_scatter | solution.py:39
  364.3 233.1 %all-reduce.6.cloned.1.call-done = f32[160,16,16]{0,2,1:T(8,128)} async-done(((f32[160,16,16]{0,2,1:T(8,128)}), f32[160,16,16]{0,2,1:T(8,128)}) %all-reduce.6.cloned.1.call-update) | async-done | bytes 163856 | tf_op jit(solution)/shard_map/psum | solution.py:164
  603.6 16.7 %reduce-scatter.15.cloned.1.call-done = f32[1,1,1,64,1,512]{5,3,2,1,0,4:T(8,128)} async-done(((f32[1,2,1,64,1,512]{5,3,2,1,0,4:T(8,128)}), f32[1,1,1,64,1,512]{5,3,2,1,0,4:T(8,128)}) %reduce-scatter.15.cloned.1.call-update) | async-done | bytes 131088 | tf_op jit(solution)/shard_map/reduce_scatter | solution.py:40
  620.3 23.2 %reduce-scatter.11.cloned.1.call-done = f32[1,1,1,16,1,2048]{5,3,4,2,1,0:T(8,128)} async-done(((f32[1,2,1,16,1,2048]{5,3,4,2,1,0:T(8,128)}), f32[1,1,1,16,1,2048]{5,3,4,2,1,0:T(8,128)}) %reduce-scatter.11.cloned.1.call-update) | async-done | bytes 131088 | tf_op jit(solution)/shard_map/reduce_scatter | solution.py:40
  (84 shorter events, 57.2 us)
Async XLA Ops:
  7.2 73.8 %copy-start = (bf16[256,512]{1,0:T(8,128)(2,1)S(1)}, bf16[256,512]{1,0:T(8,128)(2,1)}, u32[]{:S(2)}) copy-start(bf16[256,512]{1,0:T(8,128)(2,1)} %param.6) | copy-start | bytes 786436
  7.2 48.8 %all-gather.13.cloned.1.call-start = ((), (), s32[]{:S(2)}) async-start(), calls=%async_computation.19 | async-start | bytes 1179648 | tf_op jit(solution)/shard_map/all_gather | solution.py:49
  13.6 67.3 %all-gather.9.cloned.1.call-start = ((), (), s32[]{:S(2)}) async-start(), calls=%async_computation.12 | async-start | bytes 3145728 | tf_op jit(solution)/shard_map/all_gather | solution.py:50
  56.0 64.5 %all-gather.15.cloned.1.call-start = ((), (), s32[]{:S(2)}) async-start(), calls=%async_computation.20 | async-start | bytes 1179648 | tf_op jit(solution)/shard_map/all_gather | solution.py:49
  62.3 3.5 copy-start.9
  66.9 17.5 %all-to-all-start.4 = ((bf16[256,4,4,32]{0,3,1,2:T(8,128)(2,1)}), bf16[256,4,4,32]{0,3,1,2:T(8,128)(2,1)S(1)}, u32[]{:S(2)}, u32[]{:S(2)}) async-start(bf16[256,4,4,32]{0,3,1,2:T(8,128)(2,1)} %copy.90), calls=%async_computation.4 | async-start | bytes 524288 | tf_op jit(solution)/shard_map/all_to_all | solution.py:27
  84.4 37.0 %all-to-all-start = ((bf16[256,4,4,128]{0,3,1,2:T(8,128)(2,1)}), bf16[256,4,4,128]{0,3,1,2:T(8,128)(2,1)S(1)}, u32[]{:S(2)}, u32[]{:S(2)}) async-start(bf16[256,4,4,128]{0,3,1,2:T(8,128)(2,1)} %copy.81), calls=%async_computation | async-start | bytes 2097152 | tf_op jit(solution)/shard_map/all_to_all | solution.py:27
  87.9 57.4 %all-gather.11.cloned.1.call-start = ((), (), s32[]{:S(2)}) async-start(), calls=%async_computation.13 | async-start | bytes 3145728 | tf_op jit(solution)/shard_map/all_gather | solution.py:50
  121.3 14.4 %all-to-all-start.5 = ((bf16[256,4,4,32]{0,3,2,1:T(8,128)(2,1)}), bf16[256,4,4,32]{0,3,2,1:T(8,128)(2,1)S(1)}, u32[]{:S(2)}, u32[]{:S(2)}) async-start(bf16[256,4,4,32]{0,3,2,1:T(8,128)(2,1)} %copy.91), calls=%async_computation.5 | async-start | bytes 524288 | tf_op jit(solution)/shard_map/all_to_all | solution.py:28
  127.8 12.2 %copy-start.11 = (bf16[128,16,16]{0,2,1:T(8,128)(2,1)S(1)}, bf16[128,16,16]{0,2,1:T(8,128)(2,1)}, u32[]{:S(2)}) copy-start(bf16[128,16,16]{0,2,1:T(8,128)(2,1)} %param.8) | copy-start | bytes 196612
  135.7 30.0 %all-to-all-start.1 = ((bf16[256,4,4,128]{0,3,2,1:T(8,128)(2,1)}), bf16[256,4,4,128]{0,3,2,1:T(8,128)(2,1)}, u32[]{:S(2)}, u32[]{:S(2)}) async-start(bf16[256,4,4,128]{0,3,2,1:T(8,128)(2,1)} %copy.82), calls=%async_computation.1 | async-start | bytes 2097152 | tf_op jit(solution)/shard_map/all_to_all | solution.py:28
  165.7 5.5 copy-start.7
  187.3 7.6 %copy-start.8 = (bf16[256,16,128]{0,1,2:T(8,128)(2,1)S(1)}, bf16[256,16,128]{0,1,2:T(8,128)(2,1)}, u32[]{:S(2)}) copy-start(bf16[256,16,128]{0,1,2:T(8,128)(2,1)} %get-tuple-element.21) | copy-start | bytes 3145732
  188.4 26.3 %all-to-all-start.7 = ((bf16[256,4,4,128]{0,3,2,1:T(8,128)(2,1)}), bf16[256,4,4,128]{0,3,2,1:T(8,128)(2,1)S(1)}, u32[]{:S(2)}, u32[]{:S(2)}) async-start(bf16[256,4,4,128]{0,3,2,1:T(8,128)(2,1)} %copy.96), calls=%async_computation.7 | async-start | bytes 2097152 | tf_op jit(solution)/shard_map/all_to_all | solution.py:28
  194.9 76.8 %all-reduce.8.cloned.1.call-start = ((), (), s32[]{:S(2)}) async-start(), calls=%async_computation.21 | async-start | bytes 16777216
  217.4 99.6 %reduce-scatter.13.cloned.1.call-start = ((), (), s32[]{:S(2)}) async-start(), calls=%async_computation.17 | async-start | bytes 2359296 | tf_op jit(solution)/shard_map/reduce_scatter | solution.py:39
  275.6 87.7 %reduce-scatter.9.cloned.1.call-start = ((), (), s32[]{:S(2)}) async-start(), calls=%async_computation.14 | async-start | bytes 2359296 | tf_op jit(solution)/shard_map/reduce_scatter | solution.py:39
  283.1 17.4 %copy-start.3 = (bf16[256,16,128]{0,1,2:T(8,128)(2,1)S(1)}, bf16[256,16,128]{0,1,2:T(8,128)(2,1)}, u32[]{:S(2)}) copy-start(bf16[256,16,128]{0,1,2:T(8,128)(2,1)} %copy-done.2) | copy-start | bytes 3145732
  293.1 14.8 %all-to-all-start.3 = ((bf16[256,4,4,32]{0,3,2,1:T(8,128)(2,1)}), bf16[256,4,4,32]{0,3,2,1:T(8,128)(2,1)S(1)}, u32[]{:S(2)}, u32[]{:S(2)}) async-start(bf16[256,4,4,32]{0,3,2,1:T(8,128)(2,1)} %copy.88), calls=%async_computation.3 | async-start | bytes 524288 | tf_op jit(solution)/shard_map/all_to_all | solution.py:28
  299.6 297.9 %all-reduce.6.cloned.1.call-start = ((), (), s32[]{:S(2)}) async-start(), calls=%async_computation.16 | async-start | bytes 524288 | tf_op jit(solution)/shard_map/psum | solution.py:164
  300.4 7.5 %copy-start.10 = (bf16[256,512]{0,1:T(8,128)(2,1)S(1)}, bf16[256,512]{0,1:T(8,128)(2,1)}, u32[]{:S(2)}) copy-start(bf16[256,512]{0,1:T(8,128)(2,1)} %copy.99) | copy-start | bytes 786436
  302.9 297.7 %copy-start.5 = (bf16[256,4,4,128]{0,3,2,1:T(8,128)(2,1)S(1)}, bf16[256,4,4,128]{0,3,2,1:T(8,128)(2,1)}, u32[]{:S(2)}) copy-start(bf16[256,4,4,128]{0,3,2,1:T(8,128)(2,1)} %copy-done.4) | copy-start | bytes 3145732
  309.3 311.0 %reduce-scatter.15.cloned.1.call-start = ((), (), s32[]{:S(2)}) async-start(), calls=%async_computation.18 | async-start | bytes 393216 | tf_op jit(solution)/shard_map/reduce_scatter | solution.py:40
  317.0 326.5 %reduce-scatter.11.cloned.1.call-start = ((), (), s32[]{:S(2)}) async-start(), calls=%async_computation.15 | async-start | bytes 393216 | tf_op jit(solution)/shard_map/reduce_scatter | solution.py:40
  (4 other events, 6.4 us)
Sparse Core Ops, SparseCore 0:
  13.7 42.2 all-gather.12
  58.1 22.8 all-gather.8
  83.0 37.5 all-gather.14
  122.5 22.7 all-gather.10
  217.5 54.1 all-reduce.7
  275.7 41.1 reduce-scatter.12
  319.8 43.4 reduce-scatter.8
  366.7 230.6 all-reduce.5
  601.0 19.2 reduce-scatter.14
  623.5 19.9 reduce-scatter.10
where the time goes:
time: 652 us; the launch traced here: 650 us
  waiting for transfers between devices  509 us (78%)
  blocking collectives  35.8 us (5%)
  local copies, waits for them, and re-layouts  33.3 us (5%)
  starting transfers between devices  31.5 us (5%)
  matrix products  23.7 us (4%)
  between operations  14.3 us (2%)
    psum x1, waiting for transfers between devices, on_device(): rights = lax.psum(rights, DP_AXES)  233 us
    all_gather x2, waiting for transfers between devices, dp_all_gather(): x = lax.all_gather(x, 'z', axis=row_axis, tiled=True)  75 us
    reduce_scatter x2, waiting for transfers between devices, dp_reduce_scatter(): x = lax.psum_scatter(x, 'z', scatter_dimension=row_axis, tiled=True)  53.9 us
    unnamed x11, waiting for transfers between devices  53.1 us
    all_to_all x4, waiting for transfers between devices, exchange(): shaped = lax.all_to_all(shaped, 'yhi', 1, 1, tiled=True)  40.3 us
    reduce_scatter x2, waiting for transfers between devices, dp_reduce_scatter(): x = lax.psum_scatter(x, 'ylo', scatter_dimension=row_axis + 1, tiled=True)  39.8 us
    all_to_all x2, blocking collectives, exchange(): shaped = lax.all_to_all(shaped, 'x', 2, 2, tiled=True)  24.2 us
    all_to_all x4, starting transfers between devices, exchange(): shaped = lax.all_to_all(shaped, 'yhi', 1, 1, tiled=True)  23.7 us
  transfers between devices with their start and end apart: 16, of which 14 were waited for; matrix products, arithmetic and copies ran while one was open for 7% of the time, Pallas kernels for 0%

commit v1 on v0

--- a/solution.py
+++ b/solution.py
@@ -9,6 +9,11 @@
 TILE_DOWN = 32
 DP_AXES = ("z", "ylo", "core")
 FEAT_AXES = ("yhi", "x")
+
+
+def _run_heads(z_in):
+    field_out = jax.lax.psum(jax.lax.psum(z_in, "z"), ("ylo", "core"))
+    return field_out
 
 
 def split_mesh(mesh):
@@ -161,7 +166,7 @@
         0,
     ).transpose(1, 0, 2)
     rights = jnp.concatenate([right_up_term, right_down_term], axis=0)
-    rights = lax.psum(rights, DP_AXES)
+    rights = _run_heads(rights)
     grad_up_right = rights[:group_up]
     grad_down_right = rights[group_up:]
     return (layer_out, grad_tokens, grad_up_left, grad_up_right, grad_down_left, grad_down_right)

time: 652 us -> 549 us (0.84)
  waiting for transfers between devices: 509 us -> 410 us
    psum x1 -> x2, waiting for transfers between devices: 233 us -> 120 us  [_run_heads(): field_out = jax.lax.psum(jax.lax.psum(z_in, 'z'), ('ylo', 'core'))]
    reduce_scatter x2, waiting for transfers between devices: 53.9 us -> 93.8 us  [dp_reduce_scatter(): x = lax.psum_scatter(x, 'z', scatter_dimension=row_axis, tiled=True)]
    unnamed x11 -> x12, waiting for transfers between devices: 53.1 us -> 29 us
  transfers between devices with their start and end apart: 16 -> 17, of which waited for: 14 -> 15; matrix products, arithmetic and copies ran while one was open for 7% -> 8% of each run, Pallas kernels for 0% -> 0%
where the time goes in v1:
time: 549 us; the launch traced here: 548 us
  waiting for transfers between devices  410 us (75%)
  blocking collectives  34.7 us (6%)
  local copies, waits for them, and re-layouts  33.3 us (6%)
  starting transfers between devices  29.1 us (5%)
  matrix products  24 us (4%)
  between operations  14.1 us (3%)
    psum x2, waiting for transfers between devices, _run_heads(): field_out = jax.lax.psum(jax.lax.psum(z_in, 'z'), ('ylo', 'core'))  120 us
    reduce_scatter x2, waiting for transfers between devices, dp_reduce_scatter(): x = lax.psum_scatter(x, 'z', scatter_dimension=row_axis, tiled=True)  93.8 us
    all_gather x2, waiting for transfers between devices, dp_all_gather(): x = lax.all_gather(x, 'z', axis=row_axis, tiled=True)  75 us
    reduce_scatter x2, waiting for transfers between devices, dp_reduce_scatter(): x = lax.psum_scatter(x, 'ylo', scatter_dimension=row_axis + 1, tiled=True)  40 us
    all_to_all x4, waiting for transfers between devices, exchange(): shaped = lax.all_to_all(shaped, 'yhi', 1, 1, tiled=True)  38.2 us
    unnamed x12, waiting for transfers between devices  29 us
    all_to_all x2, blocking collectives, exchange(): shaped = lax.all_to_all(shaped, 'x', 2, 2, tiled=True)  23.1 us
    all_to_all x4, starting transfers between devices, exchange(): shaped = lax.all_to_all(shaped, 'yhi', 1, 1, tiled=True)  21.3 us
  transfers between devices with their start and end apart: 17, of which 15 were waited for; matrix products, arithmetic and copies ran while one was open for 8% of the time, Pallas kernels for 0%

profile of v1, /device:TPU:1, one launch (start us, length us, event | category | flops | bytes accessed | tf_op | source)
XLA Modules:
  0.0 547.8 jit_solution(15136318549710244127)
XLA Ops:
  7.2 6.3 %all-gather = bf16[2,16,2048]{2,1,0:T(8,128)(2,1)} all-gather(bf16[1,16,2048]{2,1,0:T(8,128)(2,1)} %param.7), channel_id=2, replica_groups=mesh['z'=8,'ylo'=2,'core'=2,'yhi'=4,'x'=4] {'ylo'}, dimensions={0}, use_global_device_ids=true | all-gather | bytes 196608 | tf_op jit(solution)/shard_map/all_gather | solution.py:53
  13.6 42.4 %all-gather.13.cloned.1.call-done = bf16[16,16,2048]{2,1,0:T(8,128)(2,1)} async-done(((bf16[2,16,2048]{2,1,0:T(8,128)(2,1)}), bf16[16,16,2048]{2,1,0:T(8,128)(2,1)}) %all-gather.13.cloned.1.call-update) | async-done | bytes 1048592 | tf_op jit(solution)/shard_map/all_gather | solution.py:54
  56.1 5.3 all-gather.2
  70.8 10.1 %all-gather.9.cloned.1.call-done = bf16[1,8,2,2,16,2048]{5,4,3,2,1,0:T(8,128)(2,1)} async-done(((bf16[1,8,2,1,16,2048]{5,4,3,2,1,0:T(8,128)(2,1)}), bf16[1,8,2,2,16,2048]{5,4,3,2,1,0:T(8,128)(2,1)}) %all-gather.9.cloned.1.call-update) | async-done | bytes 2097168 | tf_op jit(solution)/shard_map/all_gather | solution.py:55
  87.9 32.6 %all-gather.15.cloned.1.call-done = bf16[16,64,512]{2,1,0:T(8,128)(2,1)} async-done(((bf16[2,64,512]{2,1,0:T(8,128)(2,1)}), bf16[16,64,512]{2,1,0:T(8,128)(2,1)}) %all-gather.15.cloned.1.call-update) | async-done | bytes 1048592 | tf_op jit(solution)/shard_map/all_gather | solution.py:54
  121.3 6.5 %all-to-all-start.5 = ((bf16[256,4,4,32]{0,3,2,1:T(8,128)(2,1)}), bf16[256,4,4,32]{0,3,2,1:T(8,128)(2,1)S(1)}, u32[]{:S(2)}, u32[]{:S(2)}) async-start(bf16[256,4,4,32]{0,3,2,1:T(8,128)(2,1)} %copy.91), calls=%async_computation.5 | async-start | bytes 524288 | tf_op jit(solution)/shard_map/all_to_all | solution.py:33
  128.8 6.9 %all-to-all-done.5 = bf16[256,4,4,32]{0,3,2,1:T(8,128)(2,1)S(1)} async-done(((bf16[256,4,4,32]{0,3,2,1:T(8,128)(2,1)}), bf16[256,4,4,32]{0,3,2,1:T(8,128)(2,1)S(1)}, u32[]{:S(2)}, u32[]{:S(2)}) %all-to-all-start.5) | async-done | bytes 262176 | tf_op jit(solution)/shard_map/all_to_all | solution.py:33
  135.7 4.2 all-to-all-start.1
  141.1 4.2 all-gather.11.cloned.1.call-done
  147.6 18.1 %all-to-all-done.1 = bf16[256,4,4,128]{0,3,2,1:T(8,128)(2,1)} async-done(((bf16[256,4,4,128]{0,3,2,1:T(8,128)(2,1)}), bf16[256,4,4,128]{0,3,2,1:T(8,128)(2,1)}, u32[]{:S(2)}, u32[]{:S(2)}) %all-to-all-start.1) | async-done | bytes 1048608 | tf_op jit(solution)/shard_map/all_to_all | solution.py:33
  165.7 4.5 fusion.7
  172.2 15.0 %all_to_all.40 = bf16[256,4,4,128]{0,3,1,2:T(8,128)(2,1)S(1)} all-to-all(bf16[256,4,4,128]{0,3,1,2:T(8,128)(2,1)S(1)} %copy.95), channel_id=1, replica_groups=mesh['z'=8,'ylo'=2,'core'=2,'yhi'=4,'x'=4] {'x'}, dimensions={2} | all-to-all | bytes 2097152 | tf_op jit(solution)/shard_map/all_to_all | solution.py:32
  188.3 6.5 %all-to-all-start.7 = ((bf16[256,4,4,128]{0,3,2,1:T(8,128)(2,1)}), bf16[256,4,4,128]{0,3,2,1:T(8,128)(2,1)S(1)}, u32[]{:S(2)}, u32[]{:S(2)}) async-start(bf16[256,4,4,128]{0,3,2,1:T(8,128)(2,1)} %copy.96), calls=%async_computation.7 | async-start | bytes 2097152 | tf_op jit(solution)/shard_map/all_to_all | solution.py:33
  199.0 5.4 copy.103
  204.5 10.1 %all-to-all-done.7 = bf16[256,4,4,128]{0,3,2,1:T(8,128)(2,1)S(1)} async-done(((bf16[256,4,4,128]{0,3,2,1:T(8,128)(2,1)}), bf16[256,4,4,128]{0,3,2,1:T(8,128)(2,1)S(1)}, u32[]{:S(2)}, u32[]{:S(2)}) %all-to-all-start.7) | async-done | bytes 1048608 | tf_op jit(solution)/shard_map/all_to_all | solution.py:33
  221.0 8.0 %all_to_all.41 = bf16[256,4,4,32]{0,3,1,2:T(8,128)(2,1)S(1)} all-to-all(bf16[256,4,4,32]{0,3,1,2:T(8,128)(2,1)S(1)} %copy.87), channel_id=1, replica_groups=mesh['z'=8,'ylo'=2,'core'=2,'yhi'=4,'x'=4] {'x'}, dimensions={2} | all-to-all | bytes 524288 | tf_op jit(solution)/shard_map/all_to_all | solution.py:32
  229.8 4.1 all-to-all-start.3
  243.1 28.8 %all-reduce.11.cloned.1.call-done = (f32[8,2,2,16,1,2048]{5,3,4,2,1,0:T(8,128)}, f32[8,2,2,64,1,512]{5,3,2,1,0,4:T(8,128)}) async-done(((f32[8,2,2,16,1,2048]{5,3,4,2,1,0:T(8,128)}, f32[8,2,2,64,1,512]{5,3,2,1,0,4:T(8,128)}), (f32[8,2,2,16,1,2048]{5,3,4,2,1,0:T(8,128)}, f32[8,2,2,64,1,512]{5,3,2,1,0,4:T(8,128)})) %all-reduce.11.cloned.1.call-update) | async-done | bytes 8388624
  279.9 68.8 %all-reduce.7.cloned.1.call-done = f32[160,16,16]{0,2,1:T(8,128)} async-done(((f32[160,16,16]{0,2,1:T(8,128)}), f32[160,16,16]{0,2,1:T(8,128)}) %all-reduce.7.cloned.1.call-update) | async-done | bytes 163856 | tf_op jit(solution)/shard_map/psum | solution.py:15
  348.7 47.0 %reduce-scatter.13.cloned.1.call-done = f32[1,2,1,64,1,512]{5,3,2,1,0,4:T(8,128)} async-done(((f32[8,2,1,64,1,512]{5,3,2,1,0,4:T(8,128)}), f32[1,2,1,64,1,512]{5,3,2,1,0,4:T(8,128)}) %reduce-scatter.13.cloned.1.call-update) | async-done | bytes 262160 | tf_op jit(solution)/shard_map/reduce_scatter | solution.py:44
  395.8 46.8 %reduce-scatter.9.cloned.1.call-done = f32[1,2,1,16,1,2048]{5,3,4,2,1,0:T(8,128)} async-done(((f32[8,2,1,16,1,2048]{5,3,4,2,1,0:T(8,128)}), f32[1,2,1,16,1,2048]{5,3,4,2,1,0:T(8,128)}) %reduce-scatter.9.cloned.1.call-update) | async-done | bytes 262160 | tf_op jit(solution)/shard_map/reduce_scatter | solution.py:44
  443.7 51.3 %all-reduce.9.cloned.1.call-done = f32[160,16,16]{0,2,1:T(8,128)} async-done(((f32[160,16,16]{0,2,1:T(8,128)}), f32[160,16,16]{0,2,1:T(8,128)}) %all-reduce.9.cloned.1.call-update) | async-done | bytes 163856 | tf_op jit(solution)/shard_map/psum | solution.py:15
  501.2 16.5 %reduce-scatter.15.cloned.1.call-done = f32[1,1,1,64,1,512]{5,3,2,1,0,4:T(8,128)} async-done(((f32[1,2,1,64,1,512]{5,3,2,1,0,4:T(8,128)}), f32[1,1,1,64,1,512]{5,3,2,1,0,4:T(8,128)}) %reduce-scatter.15.cloned.1.call-update) | async-done | bytes 131088 | tf_op jit(solution)/shard_map/reduce_scatter | solution.py:45
  517.7 23.6 %reduce-scatter.11.cloned.1.call-done = f32[1,1,1,16,1,2048]{5,3,4,2,1,0:T(8,128)} async-done(((f32[1,2,1,16,1,2048]{5,3,4,2,1,0:T(8,128)}), f32[1,1,1,16,1,2048]{5,3,4,2,1,0:T(8,128)}) %reduce-scatter.11.cloned.1.call-update) | async-done | bytes 131088 | tf_op jit(solution)/shard_map/reduce_scatter | solution.py:45
  (87 shorter events, 60.6 us)
Async XLA Ops:
  7.2 73.8 %copy-start = (bf16[256,512]{1,0:T(8,128)(2,1)S(1)}, bf16[256,512]{1,0:T(8,128)(2,1)}, u32[]{:S(2)}) copy-start(bf16[256,512]{1,0:T(8,128)(2,1)} %param.6) | copy-start | bytes 786436
  7.2 48.8 %all-gather.13.cloned.1.call-start = ((), (), s32[]{:S(2)}) async-start(), calls=%async_computation.20 | async-start | bytes 1179648 | tf_op jit(solution)/shard_map/all_gather | solution.py:54
  13.6 67.3 %all-gather.9.cloned.1.call-start = ((), (), s32[]{:S(2)}) async-start(), calls=%async_computation.12 | async-start | bytes 3145728 | tf_op jit(solution)/shard_map/all_gather | solution.py:55
  56.0 64.5 %all-gather.15.cloned.1.call-start = ((), (), s32[]{:S(2)}) async-start(), calls=%async_computation.21 | async-start | bytes 1179648 | tf_op jit(solution)/shard_map/all_gather | solution.py:54
  66.9 17.5 %all-to-all-start.4 = ((bf16[256,4,4,32]{0,3,1,2:T(8,128)(2,1)}), bf16[256,4,4,32]{0,3,1,2:T(8,128)(2,1)S(1)}, u32[]{:S(2)}, u32[]{:S(2)}) async-start(bf16[256,4,4,32]{0,3,1,2:T(8,128)(2,1)} %copy.90), calls=%async_computation.4 | async-start | bytes 524288 | tf_op jit(solution)/shard_map/all_to_all | solution.py:32
  84.4 36.9 %all-to-all-start = ((bf16[256,4,4,128]{0,3,1,2:T(8,128)(2,1)}), bf16[256,4,4,128]{0,3,1,2:T(8,128)(2,1)S(1)}, u32[]{:S(2)}, u32[]{:S(2)}) async-start(bf16[256,4,4,128]{0,3,1,2:T(8,128)(2,1)} %copy.81), calls=%async_computation | async-start | bytes 2097152 | tf_op jit(solution)/shard_map/all_to_all | solution.py:32
  87.9 57.4 %all-gather.11.cloned.1.call-start = ((), (), s32[]{:S(2)}) async-start(), calls=%async_computation.13 | async-start | bytes 3145728 | tf_op jit(solution)/shard_map/all_gather | solution.py:55
  121.3 14.4 %all-to-all-start.5 = ((bf16[256,4,4,32]{0,3,2,1:T(8,128)(2,1)}), bf16[256,4,4,32]{0,3,2,1:T(8,128)(2,1)S(1)}, u32[]{:S(2)}, u32[]{:S(2)}) async-start(bf16[256,4,4,32]{0,3,2,1:T(8,128)(2,1)} %copy.91), calls=%async_computation.5 | async-start | bytes 524288 | tf_op jit(solution)/shard_map/all_to_all | solution.py:33
  127.8 12.2 %copy-start.11 = (bf16[128,16,16]{0,2,1:T(8,128)(2,1)S(1)}, bf16[128,16,16]{0,2,1:T(8,128)(2,1)}, u32[]{:S(2)}) copy-start(bf16[128,16,16]{0,2,1:T(8,128)(2,1)} %param.8) | copy-start | bytes 196612
  135.7 30.0 %all-to-all-start.1 = ((bf16[256,4,4,128]{0,3,2,1:T(8,128)(2,1)}), bf16[256,4,4,128]{0,3,2,1:T(8,128)(2,1)}, u32[]{:S(2)}, u32[]{:S(2)}) async-start(bf16[256,4,4,128]{0,3,2,1:T(8,128)(2,1)} %copy.82), calls=%async_computation.1 | async-start | bytes 2097152 | tf_op jit(solution)/shard_map/all_to_all | solution.py:33
  165.7 5.5 copy-start.7
  187.2 7.6 %copy-start.8 = (bf16[256,16,128]{0,1,2:T(8,128)(2,1)S(1)}, bf16[256,16,128]{0,1,2:T(8,128)(2,1)}, u32[]{:S(2)}) copy-start(bf16[256,16,128]{0,1,2:T(8,128)(2,1)} %get-tuple-element.21) | copy-start | bytes 3145732
  188.3 26.3 %all-to-all-start.7 = ((bf16[256,4,4,128]{0,3,2,1:T(8,128)(2,1)}), bf16[256,4,4,128]{0,3,2,1:T(8,128)(2,1)S(1)}, u32[]{:S(2)}, u32[]{:S(2)}) async-start(bf16[256,4,4,128]{0,3,2,1:T(8,128)(2,1)} %copy.96), calls=%async_computation.7 | async-start | bytes 2097152 | tf_op jit(solution)/shard_map/all_to_all | solution.py:33
  194.8 77.1 %all-reduce.11.cloned.1.call-start = ((), (), s32[]{:S(2)}) async-start(), calls=%async_computation.22 | async-start | bytes 16777216
  220.8 15.1 %copy-start.3 = (bf16[256,16,128]{0,1,2:T(8,128)(2,1)S(1)}, bf16[256,16,128]{0,1,2:T(8,128)(2,1)}, u32[]{:S(2)}) copy-start(bf16[256,16,128]{0,1,2:T(8,128)(2,1)} %copy-done.2) | copy-start | bytes 3145732
  229.8 12.0 %all-to-all-start.3 = ((bf16[256,4,4,32]{0,3,2,1:T(8,128)(2,1)}), bf16[256,4,4,32]{0,3,2,1:T(8,128)(2,1)S(1)}, u32[]{:S(2)}, u32[]{:S(2)}) async-start(bf16[256,4,4,32]{0,3,2,1:T(8,128)(2,1)} %copy.88), calls=%async_computation.3 | async-start | bytes 524288 | tf_op jit(solution)/shard_map/all_to_all | solution.py:33
  233.8 114.8 %all-reduce.7.cloned.1.call-start = ((), (), s32[]{:S(2)}) async-start(), calls=%async_computation.16 | async-start | bytes 524288 | tf_op jit(solution)/shard_map/psum | solution.py:15
  236.0 5.8 %copy-start.10 = (bf16[256,512]{0,1:T(8,128)(2,1)S(1)}, bf16[256,512]{0,1:T(8,128)(2,1)}, u32[]{:S(2)}) copy-start(bf16[256,512]{0,1:T(8,128)(2,1)} %copy.99) | copy-start | bytes 786436
  243.1 152.7 %reduce-scatter.13.cloned.1.call-start = ((), (), s32[]{:S(2)}) async-start(), calls=%async_computation.18 | async-start | bytes 2359296 | tf_op jit(solution)/shard_map/reduce_scatter | solution.py:44
  275.9 166.8 %reduce-scatter.9.cloned.1.call-start = ((), (), s32[]{:S(2)}) async-start(), calls=%async_computation.14 | async-start | bytes 2359296 | tf_op jit(solution)/shard_map/reduce_scatter | solution.py:44
  279.8 218.4 %copy-start.5 = (bf16[256,4,4,128]{0,3,2,1:T(8,128)(2,1)S(1)}, bf16[256,4,4,128]{0,3,2,1:T(8,128)(2,1)}, u32[]{:S(2)}) copy-start(bf16[256,4,4,128]{0,3,2,1:T(8,128)(2,1)} %copy-done.4) | copy-start | bytes 3145732
  279.8 215.2 %all-reduce.9.cloned.1.call-start = ((), (), s32[]{:S(2)}) async-start(), calls=%async_computation.17 | async-start | bytes 524288 | tf_op jit(solution)/shard_map/psum | solution.py:15
  348.7 169.0 %reduce-scatter.15.cloned.1.call-start = ((), (), s32[]{:S(2)}) async-start(), calls=%async_computation.19 | async-start | bytes 393216 | tf_op jit(solution)/shard_map/reduce_scatter | solution.py:45
  395.8 145.5 %reduce-scatter.11.cloned.1.call-start = ((), (), s32[]{:S(2)}) async-start(), calls=%async_computation.15 | async-start | bytes 393216 | tf_op jit(solution)/shard_map/reduce_scatter | solution.py:45
  (5 other events, 9.8 us)
Sparse Core Ops, SparseCore 0:
  13.7 42.2 all-gather.12
  58.1 22.8 all-gather.8
  83.0 37.5 all-gather.14
  122.5 22.7 all-gather.10
  217.4 54.4 all-reduce.10
  274.7 73.9 all-reduce.6
  351.7 43.9 reduce-scatter.12
  398.8 43.7 reduce-scatter.8
  445.8 49.1 all-reduce.8
  498.2 19.4 reduce-scatter.14
  521.3 19.9 reduce-scatter.10
